TPU v7x, 32 devices: a whole 2x2x4 slice. The times are simulated.
32 devices in a mesh: member: 2 (over y), lon: 4 (over z), lev: 4 (over x, core).
Axes of the slice: x: 2, y: 2, z: 4, core: 2. Of those that a mesh axis runs over, the one named last changes fastest.
Arguments:
- latent: bfloat16 [512, 8, 512], P('lev', 'member', 'lon'), parts along dimension 1, may hold values from -9 to 9
- att_gain: float32 [512], replicated, may hold values from 0.1 to 1.9
- qkv_weight: bfloat16 [3, 512, 512], P(None, 'lev'), may hold values from -0.25 to 0.25
- out_weight: bfloat16 [512, 512], P('lev'), may hold values from -0.25 to 0.25
- stencil_weight: float32 [2, 9, 512], P(None, None, 'lev'), may hold values from -2.5 to 2.5
- block_gain: float32 [2, 512], replicated, may hold values from 0.1 to 1.9
- up_weight: bfloat16 [2, 2048, 512], P(None, 'lev'), may hold values from -0.25 to 0.25
- down_weight: bfloat16 [2, 2048, 512], P(None, 'lev'), may hold values from -0.125 to 0.125
Outputs:
- decoded: bfloat16 [512, 8, 512], P('lev', 'member', 'lon'), parts along dimension 1
There are 2 independent parts, one for each index of `member`. A program takes and returns all parts, laid end to end along the dimension named above; an argument that names none is the same for every part. Nothing has to cross between parts.
All inputs are finite; a program needn't handle non-finite values.
Results may differ from a plain program's by a relative error of at most 0.017.
Values may be sent and summed in bfloat16 or wider, within the bound.
No kernel may reach another device: no remote copies, remote signals or barrier semaphores. Data moves between devices by JAX's collectives and lax.ppermute only.
A program may use at most 64 MiB of HBM per device.

v0:
```python
import math
import jax
import jax.numpy as jnp
from jax import lax
from jax.sharding import PartitionSpec as P

C = 512
H = 8
BLOCKS = 2
attention_scale = 24.0
band_start = 30.0
grid_step = 0.25
epsilon = 1e-06


def secant_rows(count):
    rows = jnp.arange(count).astype(jnp.float32)
    return 1.0 / jnp.cos((band_start + grid_step * rows) * (math.pi / 180.0))


def norm_channels(values, gain):
    scale = lax.rsqrt(jnp.mean(values * values, axis=0, keepdims=True) + epsilon)
    return values * scale * gain[:, None, None]


def unit_heads(values):
    return values * lax.rsqrt(jnp.sum(values * values, axis=1, keepdims=True) + epsilon)


def gather_channels(values):
    return lax.all_gather(values, "lev", axis=0, tiled=True)


def scatter_sum(partial, axis):
    devices = lax.axis_size(axis)
    me = lax.axis_index(axis)
    chips, core = (devices // 2, me % 2)
    chip = me // 2
    blocks = partial.reshape(chips, 2, -1, *partial.shape[1:])
    mine = jnp.take(blocks, core, axis=1).astype(jnp.float32)
    theirs = jnp.take(blocks, 1 - core, axis=1)
    pair = mine + lax.ppermute(theirs, axis, [(i, i ^ 1) for i in range(devices)]).astype(
        jnp.float32
    )
    total = jnp.take(pair, chip, axis=0)
    for shift in range(1, chips):
        pairs = [(i, (i // 2 + shift) % chips * 2 + i % 2) for i in range(devices)]
        sent = jnp.take(pair, (chip + shift) % chips, axis=0).astype(jnp.bfloat16)
        total = total + lax.ppermute(sent, axis, pairs).astype(jnp.float32)
    return total


def spread_sum(weight, activation):
    partial = lax.dot_general(
        weight, activation, (((0,), (0,)), ((), ())), preferred_element_type=jnp.float32
    ).astype(jnp.bfloat16)
    return scatter_sum(partial, "lev")


def gather_strips(values, axis):
    devices = lax.axis_size(axis)
    pieces = [values]
    for shift in range(1, devices):
        pairs = [(i, (i + shift) % devices) for i in range(devices)]
        pieces.append(lax.ppermute(values, axis, pairs))
    return jnp.concatenate(pieces, axis=-1)


def make_fold(queries, pieces):
    key_part, value_part = pieces
    scores = (
        jnp.einsum("hdri,phdrj->hripj", queries, key_part, preferred_element_type=jnp.float32)
        * attention_scale
    )
    weights = jnp.exp(scores)
    numerator = jnp.einsum(
        "hripj,phdrj->hdri",
        weights.astype(jnp.bfloat16),
        value_part,
        preferred_element_type=jnp.float32,
    )
    return (numerator, jnp.sum(weights, axis=(3, 4)))


def block_apply(state, block_index, stencil_weight, block_gain, up_weight, down_weight):
    lat_rows = state.shape[1]
    out_cols = state.shape[2] - 2
    secants = secant_rows(lat_rows)[None, :, None]
    padded = jnp.pad(state.astype(jnp.float32), ((0, 0), (1, 1), (0, 0)))
    tap_weights = stencil_weight[block_index]
    stencil_sum = jnp.zeros((state.shape[0], lat_rows, out_cols), jnp.float32)
    for row_step in (-1, 0, 1):
        for col_step in (-1, 0, 1):
            shifted = padded[
                :, 1 + row_step : 1 + row_step + lat_rows, 1 + col_step : 1 + col_step + out_cols
            ]
            tap_row = tap_weights[3 * (row_step + 1) + col_step + 1][:, None, None]
            if col_step != 0:
                stencil_sum = stencil_sum + tap_row * secants * shifted
            else:
                stencil_sum = stencil_sum + tap_row * shifted
    smoothed = stencil_sum.astype(jnp.bfloat16)
    full_channels = gather_channels(smoothed.reshape(smoothed.shape[0], -1)).reshape(
        -1, *smoothed.shape[1:]
    )
    block_normed = norm_channels(full_channels.astype(jnp.float32), block_gain[block_index]).astype(
        jnp.bfloat16
    )
    block_normed = block_normed.reshape(full_channels.shape[0], -1)
    hidden = jax.nn.gelu(
        jnp.dot(up_weight[block_index], block_normed, preferred_element_type=jnp.float32)
    ).astype(jnp.bfloat16)
    update = spread_sum(down_weight[block_index], hidden)
    center = state[:, :, 1:-1]
    return (center.astype(jnp.float32) + update.reshape(center.shape)).astype(jnp.bfloat16)


def edges(values, width):
    return jnp.concatenate([values[..., :width], values[..., -width:]], axis=-1)


def per_device(
    latent, att_gain, qkv_weight, out_weight, stencil_weight, block_gain, up_weight, down_weight
):
    ch_local, lat_rows, columns = latent.shape
    head_size = C // H
    heads_local = qkv_weight.shape[1] // head_size
    reach = BLOCKS
    gathered = gather_channels(latent.reshape(ch_local, -1)).reshape(-1, lat_rows, columns)
    normed = norm_channels(gathered.astype(jnp.float32), att_gain).astype(jnp.bfloat16)
    projected = jnp.einsum("koc,crw->korw", qkv_weight, normed, preferred_element_type=jnp.float32)
    projected = projected.reshape(3, heads_local, head_size, lat_rows, columns)
    queries = unit_heads(projected[0]).astype(jnp.bfloat16)
    key_rows = unit_heads(projected[1]).astype(jnp.bfloat16)
    value_rows = projected[2].astype(jnp.bfloat16)
    key_value = jnp.stack([key_rows, value_rows]).reshape(-1, lat_rows, columns)
    rim = jnp.stack(
        [edges(queries.reshape(ch_local, lat_rows, columns), reach), edges(latent, reach)]
    )
    rim_rows = rim.size // (lat_rows * columns)
    payload = jnp.concatenate([key_value, rim.reshape(rim_rows, lat_rows, columns)], axis=0)
    strips = lax.axis_size("lon")
    pieces = [key_value]
    from_left = from_right = None
    for shift in range(1, strips):
        pairs = [(i, (i + shift) % strips) for i in range(strips)]
        sent = payload if shift in (1, strips - 1) else key_value
        got = lax.ppermute(sent, "lon", pairs)
        pieces.append(got[: key_value.shape[0]])
        if shift == 1:
            from_left = got[key_value.shape[0] :].reshape(rim.shape)[..., reach:]
        if shift == strips - 1:
            from_right = got[key_value.shape[0] :].reshape(rim.shape)[..., :reach]
    all_keys = jnp.stack(pieces).reshape(strips, 2, heads_local, head_size, lat_rows, columns)
    wide_queries = jnp.concatenate(
        [from_left[0], queries.reshape(ch_local, lat_rows, columns), from_right[0]], axis=-1
    ).reshape(heads_local, head_size, lat_rows, -1)
    wide_latent = jnp.concatenate([from_left[1], latent, from_right[1]], axis=-1)
    numerator, denominator = make_fold(wide_queries, (all_keys[:, 0], all_keys[:, 1]))
    attended = (numerator / denominator[:, None]).astype(jnp.bfloat16)
    update = spread_sum(out_weight, attended.reshape(ch_local, -1))
    current = (wide_latent.astype(jnp.float32) + update.reshape(wide_latent.shape)).astype(
        jnp.bfloat16
    )
    for block_index in range(BLOCKS):
        current = block_apply(
            current, block_index, stencil_weight, block_gain, up_weight, down_weight
        )
    return current


def solution(mesh):
    placed = (
        P("lev", "member", "lon"),
        P(),
        P(None, "lev", None),
        P("lev", None),
        P(None, None, "lev"),
        P(),
        P(None, "lev", None),
        P(None, "lev", None),
    )
    return jax.shard_map(
        per_device, mesh=mesh, in_specs=placed, out_specs=P("lev", "member", "lon"), check_vma=False
    )
```

profile of v0, /device:TPU:16, one launch (start us, length us, event | category | flops | bytes accessed | tf_op | source)
XLA Modules:
  0.0 84.5 jit_solution(3306220149589290437)
XLA Ops:
  0.0 1.1 %copy.88 = bf16[128,4,128]{0,2,1:T(8,128)(2,1)S(1)} copy(bf16[128,4,128]{2,1,0:T(4,128)(2,1)} %param.20) | data formatting | bytes 262144 | tf_op args[0]
  1.1 7.2 %all_gather.9 = bf16[512,512]{0,1:T(8,128)(2,1)S(1)} all-gather(bf16[128,512]{0,1:T(8,128)(2,1)S(1)} %bitcast.197), channel_id=1, replica_groups=mesh['member'=2,'lon'=4,'lev'=4] {'lev'}, dimensions={0}, use_global_device_ids=true | all-gather | bytes 655360 | tf_op jit(solution)/shard_map/all_gather | solution.py:31
  8.3 0.2 multiply_reduce_fusion
  8.5 0.5 convolution_bitcast_fusion.2
  9.0 0.1 slice_multiply_fusion.6
  9.2 0.1 fusion.129
  9.3 0.4 collective-permute-start.2
  9.8 0.1 fusion.132
  9.9 0.1 copy.96
  10.0 0.1 copy.97
  10.2 0.2 copy.100
  10.4 0.3 reshape.629
  10.8 2.8 %collective-permute-start.1 = (bf16[264,4,128]{2,0,1:T(8,128)(2,1)S(1)}, bf16[264,4,128]{2,0,1:T(8,128)(2,1)S(1)}, u32[]{:S(2)}, u32[]{:S(2)}) collective-permute-start(bf16[264,4,128]{2,0,1:T(8,128)(2,1)S(1)} %pad_maximum_fusion.1), channel_id=1, source_target_pairs={{0,12},{4,0},{8,4},{12,8},{1,13},{5,1},{9,5},{13,9},{2,14},{6,2},{... | collective-permute-start | bytes 811016 | tf_op jit(solution)/shard_map/ppermute | solution.py:148
  13.7 19.3 %collective-permute-done.1 = bf16[264,4,128]{2,0,1:T(8,128)(2,1)S(1)} collective-permute-done((bf16[264,4,128]{2,0,1:T(8,128)(2,1)S(1)}, bf16[264,4,128]{2,0,1:T(8,128)(2,1)S(1)}, u32[]{:S(2)}, u32[]{:S(2)}) %collective-permute-start.1) | collective-permute-done | bytes 270368 | tf_op jit(solution)/shard_map/ppermute | solution.py:148
  33.0 0.6 reshape.631
  33.6 0.1 slice_bitcast_fusion.4
  33.7 2.4 %collective-permute-done = bf16[264,4,128]{2,0,1:T(8,128)(2,1)S(1)} collective-permute-done((bf16[264,4,128]{2,0,1:T(8,128)(2,1)S(1)}, bf16[264,4,128]{2,0,1:T(8,128)(2,1)S(1)}, u32[]{:S(2)}, u32[]{:S(2)}) %collective-permute-start) | collective-permute-done | bytes 270368 | tf_op jit(solution)/shard_map/ppermute | solution.py:148
  36.1 0.6 reshape.630
  36.7 0.2 slice_bitcast_fusion.5
  37.0 0.1 pad_maximum_fusion
  37.1 0.9 %fusion = (f32[2,4,132]{2,1,0:T(4,128)S(1)}, f32[2,4,132,4,128]{4,2,3,1,0:T(8,128)S(1)}) fusion(bf16[4,2,2,64,4,128]{5,3,0,4,2,1:T(8,128)(2,1)S(1)} %pad_maximum_fusion, bf16[2,64,4,2]{3,1,2,0:T(8,128)(2,1)S(1)} %copy.114, bf16[2,64,4,128]{3,1,2,0:T(8,128)(2,1)S(1)} %fusion.115, bf16[2,64,4,2]{3,1,2,0:T(8,128)(2,1)S(1)} %copy.113), kind=kOutput, calls=%fused_computation.1 | convolution fusion | flops 70691808 | bytes 3084416 | tf_op jit(solution)/shard_map/hdri,phdrj->hripj/dot_general | solution.py:72
  38.0 0.0 copy-start.1
  38.0 0.5 fusion.34
  38.5 0.3 copy.115
  38.8 0.2 reshape.632
  38.9 0.3 fusion.2
  39.2 0.1 reshape.633
  39.4 1.1 %constant_dynamic-slice_fusion.3 = (bf16[2,1,128,528]{2,1,0,3:T(2,128)(2,1)S(1)}, bf16[2,1,128,528]{2,1,0,3:T(2,128)(2,1)S(1)}) fusion(bf16[2,2,128,528]{2,1,0,3:T(2,128)(2,1)S(1)} %reshape.633, s32[]{:T(128)S(6)} %select_n.94, s32[]{:T(128)S(6)} %select_n.96), kind=kLoop, calls=%fused_computation.173 | loop fusion | bytes 1081352 | tf_op jit(solution)/shard_map/jit(_take) | solution.py:40
  40.5 0.1 fusion.90
  40.5 0.0 copy-start.3
  40.6 0.1 collective-permute-start.3
  40.8 0.1 broadcast_multiply_fusion.5
  40.9 1.3 %collective-permute-done.3 = bf16[2,128,528]{1,2,0:T(8,128)(2,1)S(1)} collective-permute-done((bf16[2,128,528]{1,2,0:T(8,128)(2,1)S(1)}, bf16[2,128,528]{1,2,0:T(8,128)(2,1)S(1)}, u32[]{:S(2)}, u32[]{:S(2)}) %collective-permute-start.3) | collective-permute-done | bytes 270368 | tf_op jit(solution)/shard_map/ppermute | solution.py:42
  42.2 0.1 convert_add_fusion
  42.3 1.2 %collective-permute-start.4 = (bf16[128,528]{0,1:T(8,128)(2,1)S(1)}, bf16[128,528]{0,1:T(8,128)(2,1)S(1)}, u32[]{:S(2)}, u32[]{:S(2)}) collective-permute-start(bf16[128,528]{0,1:T(8,128)(2,1)S(1)} %bitcast_convert_fusion), channel_id=1, source_target_pairs={{0,2},{1,3},{2,0},{3,1},{4,6},{5,7},{6,4},{7,5},{8,10},{9,11},{10,... | collective-permute-start | bytes 405512 | tf_op jit(solution)/shard_map/ppermute | solution.py:49
  43.5 0.1 copy.106
  43.6 0.1 copy.104
  43.7 4.3 %collective-permute-done.4 = bf16[128,528]{0,1:T(8,128)(2,1)S(1)} collective-permute-done((bf16[128,528]{0,1:T(8,128)(2,1)S(1)}, bf16[128,528]{0,1:T(8,128)(2,1)S(1)}, u32[]{:S(2)}, u32[]{:S(2)}) %collective-permute-start.4) | collective-permute-done | bytes 135200 | tf_op jit(solution)/shard_map/ppermute | solution.py:49
  48.1 0.1 fusion.131
  48.1 0.0 copy-start.5
  48.1 0.2 fusion.84
  48.4 7.0 %all_gather.10 = bf16[512,520]{0,1:T(8,128)(2,1)S(1)} all-gather(bf16[128,520]{0,1:T(8,128)(2,1)S(1)} %reshape.635), channel_id=1, replica_groups=mesh['member'=2,'lon'=4,'lev'=4] {'lev'}, dimensions={0}, use_global_device_ids=true | all-gather | bytes 665600 | tf_op jit(solution)/shard_map/all_gather | solution.py:31
  55.4 0.2 fusion.6
  55.6 2.1 %fusion.3 = bf16[512,520]{0,1:T(8,128)(2,1)S(1)} fusion(bf16[512,520]{0,1:T(8,128)(2,1)S(1)} %all_gather.10, f32[512]{0:T(512)S(1)} %bitcast.213, f32[520]{0:T(1024)S(1)} %add_rsqrt_fusion, bf16[2,512,512]{2,1,0:T(8,128)(2,1)S(1)} %copy-done.5, bf16[2,512,512]{2,1,0:T(8,128)(2,1)} %param.26), kind=kOutput, calls=%fused_computation.16 | convolution fusion | flops 548986880 | bytes 2119680 | tf_op jit(solution)/shard_map/dot_general | solution.py:54
  57.7 0.1 reshape.636
  57.8 1.1 %constant_dynamic-slice_fusion.1 = (bf16[2,1,128,520]{2,1,0,3:T(2,128)(2,1)S(1)}, bf16[2,1,128,520]{2,1,0,3:T(2,128)(2,1)S(1)}) fusion(bf16[2,2,128,520]{2,1,0,3:T(2,128)(2,1)S(1)} %reshape.636, s32[]{:T(128)S(6)} %select_n.94, s32[]{:T(128)S(6)} %select_n.96), kind=kLoop, calls=%fused_computation.171 | loop fusion | bytes 1064968 | tf_op jit(solution)/shard_map/jit(_take) | solution.py:40
  59.0 0.4 collective-permute-start.5
  59.4 1.2 %collective-permute-done.5 = bf16[2,128,520]{1,2,0:T(8,128)(2,1)S(1)} collective-permute-done((bf16[2,128,520]{1,2,0:T(8,128)(2,1)S(1)}, bf16[2,128,520]{1,2,0:T(8,128)(2,1)S(1)}, u32[]{:S(2)}, u32[]{:S(2)}) %collective-permute-start.5) | collective-permute-done | bytes 266272 | tf_op jit(solution)/shard_map/ppermute | solution.py:42
  60.6 0.1 convert_add_fusion.1
  60.7 1.0 %collective-permute-start.6 = (bf16[128,520]{0,1:T(8,128)(2,1)S(1)}, bf16[128,520]{0,1:T(8,128)(2,1)S(1)}, u32[]{:S(2)}, u32[]{:S(2)}) collective-permute-start(bf16[128,520]{0,1:T(8,128)(2,1)S(1)} %bitcast_convert_fusion.1), channel_id=1, source_target_pairs={{0,2},{1,3},{2,0},{3,1},{4,6},{5,7},{6,4},{7,5},{8,10},{9,11},{10,... | collective-permute-start | bytes 399368 | tf_op jit(solution)/shard_map/ppermute | solution.py:49
  61.7 4.9 %collective-permute-done.6 = bf16[128,520]{0,1:T(8,128)(2,1)S(1)} collective-permute-done((bf16[128,520]{0,1:T(8,128)(2,1)S(1)}, bf16[128,520]{0,1:T(8,128)(2,1)S(1)}, u32[]{:S(2)}, u32[]{:S(2)}) %collective-permute-start.6) | collective-permute-done | bytes 133152 | tf_op jit(solution)/shard_map/ppermute | solution.py:49
  66.6 0.1 fusion.130
  66.7 0.2 fusion.103
  66.9 6.6 %all_gather.11 = bf16[512,512]{0,1:T(8,128)(2,1)S(1)} all-gather(bf16[128,512]{0,1:T(8,128)(2,1)S(1)} %bitcast.205), channel_id=1, replica_groups=mesh['member'=2,'lon'=4,'lev'=4] {'lev'}, dimensions={0}, use_global_device_ids=true | all-gather | bytes 655360 | tf_op jit(solution)/shard_map/all_gather | solution.py:31
  73.5 0.2 fusion.17
  73.7 2.1 %convolution_convert_fusion.2 = bf16[512,512]{0,1:T(8,128)(2,1)S(1)} fusion(bf16[512,512]{0,1:T(8,128)(2,1)S(1)} %all_gather.11, bf16[2,512,512]{2,1,0:T(8,128)(2,1)S(1)} %copy-done.5, bf16[2,512,512]{2,1,0:T(8,128)(2,1)} %param.26, f32[512]{0:T(512)S(1)} %bitcast.212, f32[512]{0:T(512)S(1)} %add_rsqrt_fusion.1), kind=kOutput, calls=%fused_computation.13 | convolution fusion | flops 540540928 | bytes 2101248 | tf_op jit(solution)/shard_map/dot_general | solution.py:54
  75.9 0.4 collective-permute-start.7
  76.3 1.2 %collective-permute-done.7 = bf16[2,128,512]{2,1,0:T(8,128)(2,1)S(1)} collective-permute-done((bf16[2,128,512]{2,1,0:T(8,128)(2,1)S(1)}, bf16[2,128,512]{2,1,0:T(8,128)(2,1)S(1)}, u32[]{:S(2)}, u32[]{:S(2)}) %collective-permute-start.7) | collective-permute-done | bytes 262176 | tf_op jit(solution)/shard_map/ppermute | solution.py:42
  77.5 0.1 convert_add_fusion.2
  77.6 1.2 %collective-permute-start.8 = (bf16[128,512]{1,0:T(8,128)(2,1)S(1)}, bf16[128,512]{1,0:T(8,128)(2,1)S(1)}, u32[]{:S(2)}, u32[]{:S(2)}) collective-permute-start(bf16[128,512]{1,0:T(8,128)(2,1)S(1)} %bitcast_convert_fusion.2), channel_id=1, source_target_pairs={{0,2},{1,3},{2,0},{3,1},{4,6},{5,7},{6,4},{7,5},{8,10},{9,11},{10,... | collective-permute-start | bytes 393224 | tf_op jit(solution)/shard_map/ppermute | solution.py:49
  78.8 4.6 %collective-permute-done.8 = bf16[128,512]{1,0:T(8,128)(2,1)S(1)} collective-permute-done((bf16[128,512]{1,0:T(8,128)(2,1)S(1)}, bf16[128,512]{1,0:T(8,128)(2,1)S(1)}, u32[]{:S(2)}, u32[]{:S(2)}) %collective-permute-start.8) | collective-permute-done | bytes 131104 | tf_op jit(solution)/shard_map/ppermute | solution.py:49
  83.5 0.1 copy.121
  83.6 0.1 add_convert_fusion.2
  83.7 0.8 copy.122
  (51 shorter events, 0.8 us)
Async XLA Ops:
  0.0 8.5 %copy-start = (bf16[3,128,512]{2,1,0:T(8,128)(2,1)S(1)}, bf16[3,128,512]{2,1,0:T(8,128)(2,1)}, u32[]{:S(2)}) copy-start(bf16[3,128,512]{2,1,0:T(8,128)(2,1)} %param.22) | copy-start | bytes 1179652
  0.0 8.5 %copy-start.4 = (f32[512]{0:T(512)S(1)}, f32[512]{0:T(512)}, u32[]{:S(2)}) copy-start(f32[512]{0:T(512)} %param.21) | copy-start | bytes 6148
  9.3 27.7 %collective-permute-start.2 = (bf16[256,4,128]{2,0,1:T(8,128)(2,1)S(1)}, bf16[256,4,128]{2,0,1:T(8,128)(2,1)S(1)}, u32[]{:S(2)}, u32[]{:S(2)}) collective-permute-start(bf16[256,4,128]{2,0,1:T(8,128)(2,1)S(1)} %bitcast.200), channel_id=1, source_target_pairs={{0,8},{4,12},{8,0},{12,4},{1,9},{5,13},{9,1},{13,5},{2,10},{6,14},... | collective-permute-start | bytes 786440 | tf_op jit(solution)/shard_map/ppermute | solution.py:148
  9.8 3.8 %copy-start.2 = (f32[2,9,128]{2,0,1:T(2,128)S(1)}, f32[2,9,128]{2,0,1:T(2,128)}, u32[]{:S(2)}) copy-start(f32[2,9,128]{2,0,1:T(2,128)} %param.24) | copy-start | bytes 27652
  10.8 22.2 %collective-permute-start.1 = (bf16[264,4,128]{2,0,1:T(8,128)(2,1)S(1)}, bf16[264,4,128]{2,0,1:T(8,128)(2,1)S(1)}, u32[]{:S(2)}, u32[]{:S(2)}) collective-permute-start(bf16[264,4,128]{2,0,1:T(8,128)(2,1)S(1)} %pad_maximum_fusion.1), channel_id=1, source_target_pairs={{0,12},{4,0},{8,4},{12,8},{1,13},{5,1},{9,5},{13,9},{2,14},{6,2},{... | collective-permute-start | bytes 811016 | tf_op jit(solution)/shard_map/ppermute | solution.py:148
  13.6 22.5 %collective-permute-start = (bf16[264,4,128]{2,0,1:T(8,128)(2,1)S(1)}, bf16[264,4,128]{2,0,1:T(8,128)(2,1)S(1)}, u32[]{:S(2)}, u32[]{:S(2)}) collective-permute-start(bf16[264,4,128]{2,0,1:T(8,128)(2,1)S(1)} %pad_maximum_fusion.1), channel_id=1, source_target_pairs={{0,4},{4,8},{8,12},{12,0},{1,5},{5,9},{9,13},{13,1},{2,6},{6,10},{... | collective-permute-start | bytes 811016 | tf_op jit(solution)/shard_map/ppermute | solution.py:148
  38.0 1.0 %copy-start.1 = (bf16[128,512]{1,0:T(8,128)(2,1)S(1)}, bf16[128,512]{1,0:T(8,128)(2,1)}, u32[]{:S(2)}) copy-start(bf16[128,512]{1,0:T(8,128)(2,1)} %param.23) | copy-start | bytes 393220
  40.5 2.9 %copy-start.3 = (f32[2,512]{1,0:T(2,128)S(1)}, f32[2,512]{1,0:T(2,128)}, u32[]{:S(2)}) copy-start(f32[2,512]{1,0:T(2,128)} %param.25) | copy-start | bytes 12292
  40.6 1.6 %collective-permute-start.3 = (bf16[2,128,528]{1,2,0:T(8,128)(2,1)S(1)}, bf16[2,128,528]{1,2,0:T(8,128)(2,1)S(1)}, u32[]{:S(2)}, u32[]{:S(2)}) collective-permute-start(bf16[2,128,528]{1,2,0:T(8,128)(2,1)S(1)} %fusion.90), channel_id=1, source_target_pairs={{0,1},{1,0},{2,3},{3,2},{4,5},{5,4},{6,7},{7,6},{8,9},{9,8},{10,11... | collective-permute-start | bytes 811016 | tf_op jit(solution)/shard_map/ppermute | solution.py:42
  42.3 5.7 %collective-permute-start.4 = (bf16[128,528]{0,1:T(8,128)(2,1)S(1)}, bf16[128,528]{0,1:T(8,128)(2,1)S(1)}, u32[]{:S(2)}, u32[]{:S(2)}) collective-permute-start(bf16[128,528]{0,1:T(8,128)(2,1)S(1)} %bitcast_convert_fusion), channel_id=1, source_target_pairs={{0,2},{1,3},{2,0},{3,1},{4,6},{5,7},{6,4},{7,5},{8,10},{9,11},{10,... | collective-permute-start | bytes 405512 | tf_op jit(solution)/shard_map/ppermute | solution.py:49
  48.1 7.5 %copy-start.5 = (bf16[2,512,512]{2,1,0:T(8,128)(2,1)S(1)}, bf16[2,512,512]{2,1,0:T(8,128)(2,1)}, u32[]{:S(2)}) copy-start(bf16[2,512,512]{2,1,0:T(8,128)(2,1)} %param.27) | copy-start | bytes 3145732
  59.0 1.6 %collective-permute-start.5 = (bf16[2,128,520]{1,2,0:T(8,128)(2,1)S(1)}, bf16[2,128,520]{1,2,0:T(8,128)(2,1)S(1)}, u32[]{:S(2)}, u32[]{:S(2)}) collective-permute-start(bf16[2,128,520]{1,2,0:T(8,128)(2,1)S(1)} %fusion.92), channel_id=1, source_target_pairs={{0,1},{1,0},{2,3},{3,2},{4,5},{5,4},{6,7},{7,6},{8,9},{9,8},{10,11... | collective-permute-start | bytes 798728 | tf_op jit(solution)/shard_map/ppermute | solution.py:42
  60.7 5.9 %collective-permute-start.6 = (bf16[128,520]{0,1:T(8,128)(2,1)S(1)}, bf16[128,520]{0,1:T(8,128)(2,1)S(1)}, u32[]{:S(2)}, u32[]{:S(2)}) collective-permute-start(bf16[128,520]{0,1:T(8,128)(2,1)S(1)} %bitcast_convert_fusion.1), channel_id=1, source_target_pairs={{0,2},{1,3},{2,0},{3,1},{4,6},{5,7},{6,4},{7,5},{8,10},{9,11},{10,... | collective-permute-start | bytes 399368 | tf_op jit(solution)/shard_map/ppermute | solution.py:49
  75.9 1.6 %collective-permute-start.7 = (bf16[2,128,512]{2,1,0:T(8,128)(2,1)S(1)}, bf16[2,128,512]{2,1,0:T(8,128)(2,1)S(1)}, u32[]{:S(2)}, u32[]{:S(2)}) collective-permute-start(bf16[2,128,512]{2,1,0:T(8,128)(2,1)S(1)} %select_bitcast_fusion), channel_id=1, source_target_pairs={{0,1},{1,0},{2,3},{3,2},{4,5},{5,4},{6,7},{7,6},{8,9},{9,8},{10,11... | collective-permute-start | bytes 786440 | tf_op jit(solution)/shard_map/ppermute | solution.py:42
  77.6 5.8 %collective-permute-start.8 = (bf16[128,512]{1,0:T(8,128)(2,1)S(1)}, bf16[128,512]{1,0:T(8,128)(2,1)S(1)}, u32[]{:S(2)}, u32[]{:S(2)}) collective-permute-start(bf16[128,512]{1,0:T(8,128)(2,1)S(1)} %bitcast_convert_fusion.2), channel_id=1, source_target_pairs={{0,2},{1,3},{2,0},{3,1},{4,6},{5,7},{6,4},{7,5},{8,10},{9,11},{10,... | collective-permute-start | bytes 393224 | tf_op jit(solution)/shard_map/ppermute | solution.py:49
where the time goes:
time: 84.7 us; the launch traced here: 84.5 us
  waiting for transfers between devices  39.2 us (46%)
  blocking collectives  20.9 us (25%)
  local copies, waits for them, and re-layouts  7.75 us (9%)
  starting transfers between devices  7.44 us (9%)
  matrix products  6.41 us (8%)
  other arithmetic  2.24 us (3%)
    ppermute x3, waiting for transfers between devices, per_device(): got = lax.ppermute(sent, 'lon', pairs)  21.7 us
    all_gather x3, blocking collectives, gather_channels(): return lax.all_gather(values, 'lev', axis=0, tiled=True)  20.9 us
    ppermute x3, waiting for transfers between devices, scatter_sum(): total = total + lax.ppermute(sent, axis, pairs).astype(jnp.float32)  13.8 us
    dot_general x3, matrix products, spread_sum(): lax.dot_general(weight, activation, (((0,), (0,)), ((), ())), preferred_e...  4.49 us
    ppermute x3, waiting for transfers between devices, scatter_sum(): lax.ppermute(theirs, axis, [(i, i ^ 1) for i in range(devices)])  3.69 us
    ppermute x3, starting transfers between devices, scatter_sum(): total = total + lax.ppermute(sent, axis, pairs).astype(jnp.float32)  3.34 us
    ppermute x3, starting transfers between devices, per_device(): got = lax.ppermute(sent, 'lon', pairs)  3.16 us
    another operation x2, local copies, waits for them, and re-layouts, scatter_sum(): mine = jnp.take(blocks, core, axis=1).astype(jnp.float32)  2.23 us
  transfers between devices with their start and end apart: 9, of which 8 were waited for; matrix products, arithmetic and copies ran while one was open for 4% of the time, Pallas kernels for 0%

commit v1 on v0

--- a/solution.py
+++ b/solution.py
@@ -13,6 +13,28 @@
 epsilon = 1e-06
 
 
+def in_order(parts, dim):
+    lengths = list(parts.shape[1:])
+    lengths[dim] *= parts.shape[0]
+    return jnp.moveaxis(parts, 0, dim).reshape(lengths)
+
+
+def collect(x, axis, dim):
+    peers = lax.axis_size(axis)
+    pairs = [(i, (i + 1) % peers) for i in range(peers)]
+    back = [(b, a) for a, b in pairs]
+    lower, upper = ([], [])
+    for step in range(peers - 1):
+        if step % 2 == 0:
+            lower.append(lax.ppermute(lower[-1] if lower else x, axis, pairs))
+        else:
+            upper.append(lax.ppermute(upper[-1] if upper else x, axis, back))
+    pieces = jnp.stack([*lower[::-1], x, *upper])
+    shift = lax.axis_index(axis) - len(lower)
+    pieces = pieces[(jnp.arange(peers) - shift) % peers]
+    return in_order(pieces, dim)
+
+
 def secant_rows(count):
     rows = jnp.arange(count).astype(jnp.float32)
     return 1.0 / jnp.cos((band_start + grid_step * rows) * (math.pi / 180.0))
@@ -28,7 +50,7 @@
 
 
 def gather_channels(values):
-    return lax.all_gather(values, "lev", axis=0, tiled=True)
+    return collect(values, "lev", 0)
 
 
 def scatter_sum(partial, axis):

time: 84.7 us -> 97.7 us (1.15)
  the two profiles are of different devices: /device:TPU:16 before, /device:TPU:0 now
where the time goes in v1:
time: 97.7 us; the launch traced here: 97.4 us
  waiting for transfers between devices  62.1 us (64%)
  local copies, waits for them, and re-layouts  12.5 us (13%)
  starting transfers between devices  11.8 us (12%)
  matrix products  6.16 us (6%)
  other arithmetic  4.05 us (4%)
    ppermute x6, waiting for transfers between devices, collect(): lower.append(lax.ppermute(lower[-1] if lower else x, axis, pairs))  22.6 us
    ppermute x3, waiting for transfers between devices, per_device(): got = lax.ppermute(sent, 'lon', pairs)  19.3 us
    ppermute x3, waiting for transfers between devices, scatter_sum(): total = total + lax.ppermute(sent, axis, pairs).astype(jnp.float32)  15.8 us
    ppermute x3, starting transfers between devices, collect(): upper.append(lax.ppermute(upper[-1] if upper else x, axis, back))  5.89 us
    ppermute x3, starting transfers between devices, per_device(): got = lax.ppermute(sent, 'lon', pairs)  4.73 us
    ppermute x3, waiting for transfers between devices, scatter_sum(): lax.ppermute(theirs, axis, [(i, i ^ 1) for i in range(devices)])  4.45 us
    dot_general x3, matrix products, spread_sum(): lax.dot_general(weight, activation, (((0,), (0,)), ((), ())), preferred_e...  4.36 us
    unnamed x15, local copies, waits for them, and re-layouts  2.56 us
  transfers between devices with their start and end apart: 18, of which 15 were waited for; matrix products, arithmetic and copies ran while one was open for 4% of the time, Pallas kernels for 0%

profile of v1, /device:TPU:0, one launch (start us, length us, event | category | flops | bytes accessed | tf_op | source)
XLA Modules:
  0.0 97.4 jit_solution(15247182305255891651)
XLA Ops:
  0.0 1.0 %copy.253 = bf16[16,8,4,128]{3,1,2,0:T(8,128)(2,1)S(1)} copy(bf16[16,8,4,128]{3,2,1,0:T(4,128)(2,1)} %bitcast.221) | data formatting | bytes 262144
  1.0 2.4 %collective-permute-start.2 = (bf16[128,512]{1,0:T(8,128)(2,1)S(1)}, bf16[128,512]{1,0:T(8,128)(2,1)S(1)}, u32[]{:S(2)}, u32[]{:S(2)}) collective-permute-start(bf16[128,512]{1,0:T(8,128)(2,1)S(1)} %bitcast.239), channel_id=1, source_target_pairs={{1,0},{2,1},{3,2},{0,3},{5,4},{6,5},{7,6},{4,7},{9,8},{10,9},{11,1... | collective-permute-start | bytes 393224 | tf_op jit(solution)/shard_map/ppermute | solution.py:31
  3.4 1.0 %copy.162 = bf16[128,4,128]{0,2,1:T(8,128)(2,1)S(1)} copy(bf16[128,4,128]{2,1,0:T(4,128)(2,1)} %param.20) | data formatting | bytes 262144 | tf_op args[0]
  4.5 3.9 %collective-permute-done = bf16[128,512]{1,0:T(8,128)(2,1)S(1)} collective-permute-done((bf16[128,512]{1,0:T(8,128)(2,1)S(1)}, bf16[128,512]{1,0:T(8,128)(2,1)S(1)}, u32[]{:S(2)}, u32[]{:S(2)}) %collective-permute-start) | collective-permute-done | bytes 131104 | tf_op jit(solution)/shard_map/ppermute | solution.py:29
  8.3 1.0 stack_reshape.10
  9.3 3.4 %collective-permute-done.1 = bf16[128,512]{1,0:T(8,128)(2,1)S(1)} collective-permute-done((bf16[128,512]{1,0:T(8,128)(2,1)S(1)}, bf16[128,512]{1,0:T(8,128)(2,1)S(1)}, u32[]{:S(2)}, u32[]{:S(2)}) %collective-permute-start.1) | collective-permute-done | bytes 131104 | tf_op jit(solution)/shard_map/ppermute | solution.py:29
  12.8 0.6 gather_fusion
  13.4 0.2 multiply_reduce_fusion
  13.5 0.3 reshape.1035
  13.9 0.2 copy-done.4
  14.1 1.5 %fusion.46 = bf16[512,4,128,1]{2,1,0,3:T(4,128)(2,1)S(1)} fusion(f32[512,4,128]{2,1,0:T(4,128)S(1)} %reshape.1035, f32[512]{0:T(512)S(1)} %copy-done.4, f32[4,128]{1,0:T(4,128)S(1)} %rsqrt_bitcast_fusion), kind=kLoop, calls=%fused_computation.72 | loop fusion | flops 786432 | bytes 1576960 | tf_op jit(solution)/shard_map/convert_element_type | solution.py:152
  15.6 0.4 convolution_bitcast_fusion.2
  16.2 0.1 fusion.125
  16.3 0.1 copy.160
  16.4 0.1 copy.161
  16.6 0.2 copy.164
  16.8 0.3 reshape.777
  17.3 3.7 %collective-permute-start.4 = (bf16[264,4,128]{2,0,1:T(8,128)(2,1)S(1)}, bf16[264,4,128]{2,0,1:T(8,128)(2,1)S(1)}, u32[]{:S(2)}, u32[]{:S(2)}) collective-permute-start(bf16[264,4,128]{2,0,1:T(8,128)(2,1)S(1)} %pad_maximum_fusion.4), channel_id=1, source_target_pairs={{0,12},{4,0},{8,4},{12,8},{1,13},{5,1},{9,5},{13,9},{2,14},{6,2},{... | collective-permute-start | bytes 811016 | tf_op jit(solution)/shard_map/ppermute | solution.py:170
  21.0 1.1 %collective-permute-start.5 = (bf16[256,4,128]{2,0,1:T(8,128)(2,1)S(1)}, bf16[256,4,128]{2,0,1:T(8,128)(2,1)S(1)}, u32[]{:S(2)}, u32[]{:S(2)}) collective-permute-start(bf16[256,4,128]{2,0,1:T(8,128)(2,1)S(1)} %bitcast.225), channel_id=1, source_target_pairs={{0,8},{4,12},{8,0},{12,4},{1,9},{5,13},{9,1},{13,5},{2,10},{6,14},... | collective-permute-start | bytes 786440 | tf_op jit(solution)/shard_map/ppermute | solution.py:170
  22.1 5.8 %collective-permute-done.4 = bf16[264,4,128]{2,0,1:T(8,128)(2,1)S(1)} collective-permute-done((bf16[264,4,128]{2,0,1:T(8,128)(2,1)S(1)}, bf16[264,4,128]{2,0,1:T(8,128)(2,1)S(1)}, u32[]{:S(2)}, u32[]{:S(2)}) %collective-permute-start.4) | collective-permute-done | bytes 270368 | tf_op jit(solution)/shard_map/ppermute | solution.py:170
  27.9 0.6 reshape.779
  28.5 0.1 slice_bitcast_fusion.4
  28.6 6.1 %collective-permute-done.3 = bf16[264,4,128]{2,0,1:T(8,128)(2,1)S(1)} collective-permute-done((bf16[264,4,128]{2,0,1:T(8,128)(2,1)S(1)}, bf16[264,4,128]{2,0,1:T(8,128)(2,1)S(1)}, u32[]{:S(2)}, u32[]{:S(2)}) %collective-permute-start.3) | collective-permute-done | bytes 270368 | tf_op jit(solution)/shard_map/ppermute | solution.py:170
  34.7 0.6 reshape.778
  35.3 0.2 slice_bitcast_fusion.5
  35.6 7.3 %collective-permute-done.5 = bf16[256,4,128]{2,0,1:T(8,128)(2,1)S(1)} collective-permute-done((bf16[256,4,128]{2,0,1:T(8,128)(2,1)S(1)}, bf16[256,4,128]{2,0,1:T(8,128)(2,1)S(1)}, u32[]{:S(2)}, u32[]{:S(2)}) %collective-permute-start.5) | collective-permute-done | bytes 262176 | tf_op jit(solution)/shard_map/ppermute | solution.py:170
  43.0 0.9 fusion
  43.9 0.5 fusion.34
  44.5 0.3 copy.179
  44.7 0.1 reshape.780
  44.9 0.3 fusion.2
  45.2 0.1 reshape.781
  45.3 1.1 %constant_dynamic-slice_fusion.3 = (bf16[2,1,128,528]{2,1,0,3:T(2,128)(2,1)S(1)}, bf16[2,1,128,528]{2,1,0,3:T(2,128)(2,1)S(1)}) fusion(bf16[2,2,128,528]{2,1,0,3:T(2,128)(2,1)S(1)} %reshape.781, s32[]{:T(128)S(6)} %select_n.125, s32[]{:T(128)S(6)} %select_n.127), kind=kLoop, calls=%fused_computation.179 | loop fusion | bytes 1081352 | tf_op jit(solution)/shard_map/jit(_take) | solution.py:62
  46.7 1.4 %collective-permute-done.6 = bf16[2,128,528]{1,2,0:T(8,128)(2,1)S(1)} collective-permute-done((bf16[2,128,528]{1,2,0:T(8,128)(2,1)S(1)}, bf16[2,128,528]{1,2,0:T(8,128)(2,1)S(1)}, u32[]{:S(2)}, u32[]{:S(2)}) %collective-permute-start.6) | collective-permute-done | bytes 270368 | tf_op jit(solution)/shard_map/ppermute | solution.py:64
  48.2 0.6 collective-permute-start.7
  49.0 0.1 copy.170
  49.1 0.1 copy.168
  49.2 4.7 %collective-permute-done.7 = bf16[128,528]{0,1:T(8,128)(2,1)S(1)} collective-permute-done((bf16[128,528]{0,1:T(8,128)(2,1)S(1)}, bf16[128,528]{0,1:T(8,128)(2,1)S(1)}, u32[]{:S(2)}, u32[]{:S(2)}) %collective-permute-start.7) | collective-permute-done | bytes 135200 | tf_op jit(solution)/shard_map/ppermute | solution.py:71
  54.1 0.2 fusion.75
  54.4 1.7 %collective-permute-start.10 = (bf16[128,520]{0,1:T(8,128)(2,1)S(1)}, bf16[128,520]{0,1:T(8,128)(2,1)S(1)}, u32[]{:S(2)}, u32[]{:S(2)}) collective-permute-start(bf16[128,520]{0,1:T(8,128)(2,1)S(1)} %reshape.783), channel_id=1, source_target_pairs={{1,0},{2,1},{3,2},{0,3},{5,4},{6,5},{7,6},{4,7},{9,8},{10,9},{11,1... | collective-permute-start | bytes 399368 | tf_op jit(solution)/shard_map/ppermute | solution.py:31
  56.1 3.2 %collective-permute-done.8 = bf16[128,520]{0,1:T(8,128)(2,1)S(1)} collective-permute-done((bf16[128,520]{0,1:T(8,128)(2,1)S(1)}, bf16[128,520]{0,1:T(8,128)(2,1)S(1)}, u32[]{:S(2)}, u32[]{:S(2)}) %collective-permute-start.8) | collective-permute-done | bytes 133152 | tf_op jit(solution)/shard_map/ppermute | solution.py:29
  59.4 4.3 %collective-permute-done.9 = bf16[128,520]{0,1:T(8,128)(2,1)S(1)} collective-permute-done((bf16[128,520]{0,1:T(8,128)(2,1)S(1)}, bf16[128,520]{0,1:T(8,128)(2,1)S(1)}, u32[]{:S(2)}, u32[]{:S(2)}) %collective-permute-start.9) | collective-permute-done | bytes 133152 | tf_op jit(solution)/shard_map/ppermute | solution.py:29
  63.9 0.7 gather_fusion.1
  64.5 0.2 fusion.6
  64.7 0.3 copy-done.5
  65.1 2.0 %fusion.3 = bf16[512,520]{0,1:T(8,128)(2,1)S(1)} fusion(bf16[2,512,512]{2,1,0:T(8,128)(2,1)S(1)} %copy-done.5, bf16[2,512,512]{2,1,0:T(8,128)(2,1)} %param.26, bf16[4,128,520]{1,2,0:T(8,128)(2,1)S(1)} %gather_fusion.1, f32[4,128]{1,0:T(4,128)S(1)} %bitcast.248, f32[520]{0:T(1024)S(1)} %add_rsqrt_fusion), kind=kOutput, calls=%fused_computation.19 | convolution fusion | flops 548986880 | bytes 2119680 | tf_op jit(solution)/shard_map/dot_general | solution.py:76
  67.1 0.1 reshape.784
  67.3 1.1 %constant_dynamic-slice_fusion.1 = (bf16[2,1,128,520]{2,1,0,3:T(2,128)(2,1)S(1)}, bf16[2,1,128,520]{2,1,0,3:T(2,128)(2,1)S(1)}) fusion(bf16[2,2,128,520]{2,1,0,3:T(2,128)(2,1)S(1)} %reshape.784, s32[]{:T(128)S(6)} %select_n.125, s32[]{:T(128)S(6)} %select_n.127), kind=kLoop, calls=%fused_computation.177 | loop fusion | bytes 1064968 | tf_op jit(solution)/shard_map/jit(_take) | solution.py:62
  68.5 1.5 %collective-permute-done.11 = bf16[2,128,520]{1,2,0:T(8,128)(2,1)S(1)} collective-permute-done((bf16[2,128,520]{1,2,0:T(8,128)(2,1)S(1)}, bf16[2,128,520]{1,2,0:T(8,128)(2,1)S(1)}, u32[]{:S(2)}, u32[]{:S(2)}) %collective-permute-start.11) | collective-permute-done | bytes 266272 | tf_op jit(solution)/shard_map/ppermute | solution.py:64
  70.2 5.6 %collective-permute-done.12 = bf16[128,520]{0,1:T(8,128)(2,1)S(1)} collective-permute-done((bf16[128,520]{0,1:T(8,128)(2,1)S(1)}, bf16[128,520]{0,1:T(8,128)(2,1)S(1)}, u32[]{:S(2)}, u32[]{:S(2)}) %collective-permute-start.12) | collective-permute-done | bytes 133152 | tf_op jit(solution)/shard_map/ppermute | solution.py:71
  75.9 0.2 fusion.94
  76.1 0.1 copy.199
  76.3 1.7 %collective-permute-start.15 = (bf16[128,512]{1,0:T(8,128)(2,1)S(1)}, bf16[128,512]{1,0:T(8,128)(2,1)S(1)}, u32[]{:S(2)}, u32[]{:S(2)}) collective-permute-start(bf16[128,512]{1,0:T(8,128)(2,1)S(1)} %copy.199), channel_id=1, source_target_pairs={{1,0},{2,1},{3,2},{0,3},{5,4},{6,5},{7,6},{4,7},{9,8},{10,9},{11,1... | collective-permute-start | bytes 393224 | tf_op jit(solution)/shard_map/ppermute | solution.py:31
  78.0 3.5 %collective-permute-done.13 = bf16[128,512]{1,0:T(8,128)(2,1)S(1)} collective-permute-done((bf16[128,512]{1,0:T(8,128)(2,1)S(1)}, bf16[128,512]{1,0:T(8,128)(2,1)S(1)}, u32[]{:S(2)}, u32[]{:S(2)}) %collective-permute-start.13) | collective-permute-done | bytes 131104 | tf_op jit(solution)/shard_map/ppermute | solution.py:29
  81.5 0.1 copy.200
  81.7 4.3 %collective-permute-done.14 = bf16[128,512]{1,0:T(8,128)(2,1)S(1)} collective-permute-done((bf16[128,512]{1,0:T(8,128)(2,1)S(1)}, bf16[128,512]{1,0:T(8,128)(2,1)S(1)}, u32[]{:S(2)}, u32[]{:S(2)}) %collective-permute-start.14) | collective-permute-done | bytes 131104 | tf_op jit(solution)/shard_map/ppermute | solution.py:29
  86.0 0.6 gather_fusion.2
  86.6 0.2 fusion.17
  86.7 0.2 fusion.19
  86.9 2.1 %convolution_convert_fusion.2 = bf16[512,512]{0,1:T(8,128)(2,1)S(1)} fusion(bf16[512,512]{1,0:T(8,128)(2,1)S(1)} %bitcast.231, bf16[2,512,512]{2,1,0:T(8,128)(2,1)S(1)} %copy-done.5, bf16[2,512,512]{2,1,0:T(8,128)(2,1)} %param.26), kind=kOutput, calls=%fused_computation.16 | convolution fusion | flops 539492352 | bytes 2097152 | tf_op jit(solution)/shard_map/dot_general | solution.py:76
  89.1 1.5 %collective-permute-done.16 = bf16[2,128,512]{2,1,0:T(8,128)(2,1)S(1)} collective-permute-done((bf16[2,128,512]{2,1,0:T(8,128)(2,1)S(1)}, bf16[2,128,512]{2,1,0:T(8,128)(2,1)S(1)}, u32[]{:S(2)}, u32[]{:S(2)}) %collective-permute-start.16) | collective-permute-done | bytes 262176 | tf_op jit(solution)/shard_map/ppermute | solution.py:64
  90.8 5.5 %collective-permute-done.17 = bf16[128,512]{1,0:T(8,128)(2,1)S(1)} collective-permute-done((bf16[128,512]{1,0:T(8,128)(2,1)S(1)}, bf16[128,512]{1,0:T(8,128)(2,1)S(1)}, u32[]{:S(2)}, u32[]{:S(2)}) %collective-permute-start.17) | collective-permute-done | bytes 131104 | tf_op jit(solution)/shard_map/ppermute | solution.py:71
  96.4 0.1 copy.188
  96.6 0.8 copy.189
  (82 shorter events, 2.3 us)
Async XLA Ops:
  0.0 15.6 %copy-start = (bf16[3,128,512]{2,1,0:T(8,128)(2,1)S(1)}, bf16[3,128,512]{2,1,0:T(8,128)(2,1)}, u32[]{:S(2)}) copy-start(bf16[3,128,512]{2,1,0:T(8,128)(2,1)} %param.22) | copy-start | bytes 1179652
  1.0 8.3 %collective-permute-start.2 = (bf16[128,512]{1,0:T(8,128)(2,1)S(1)}, bf16[128,512]{1,0:T(8,128)(2,1)S(1)}, u32[]{:S(2)}, u32[]{:S(2)}) collective-permute-start(bf16[128,512]{1,0:T(8,128)(2,1)S(1)} %bitcast.239), channel_id=1, source_target_pairs={{1,0},{2,1},{3,2},{0,3},{5,4},{6,5},{7,6},{4,7},{9,8},{10,9},{11,1... | collective-permute-start | bytes 393224 | tf_op jit(solution)/shard_map/ppermute | solution.py:31
  3.4 4.9 %collective-permute-start = (bf16[128,512]{1,0:T(8,128)(2,1)S(1)}, bf16[128,512]{1,0:T(8,128)(2,1)S(1)}, u32[]{:S(2)}, u32[]{:S(2)}) collective-permute-start(bf16[128,512]{1,0:T(8,128)(2,1)S(1)} %bitcast.240), channel_id=1, source_target_pairs={{0,1},{1,2},{2,3},{3,0},{4,5},{5,6},{6,7},{7,4},{8,9},{9,10},{10,1... | collective-permute-start | bytes 393224 | tf_op jit(solution)/shard_map/ppermute | solution.py:29
  8.3 4.4 %collective-permute-start.1 = (bf16[128,512]{1,0:T(8,128)(2,1)S(1)}, bf16[128,512]{1,0:T(8,128)(2,1)S(1)}, u32[]{:S(2)}, u32[]{:S(2)}) collective-permute-start(bf16[128,512]{1,0:T(8,128)(2,1)S(1)} %collective-permute-done), channel_id=1, source_target_pairs={{0,1},{1,2},{2,3},{3,0},{4,5},{5,6},{6,7},{7,4},{8,9},{9,10},{10,1... | collective-permute-start | bytes 393224 | tf_op jit(solution)/shard_map/ppermute | solution.py:29
  13.4 0.7 copy-start.4
  17.3 10.6 %collective-permute-start.4 = (bf16[264,4,128]{2,0,1:T(8,128)(2,1)S(1)}, bf16[264,4,128]{2,0,1:T(8,128)(2,1)S(1)}, u32[]{:S(2)}, u32[]{:S(2)}) collective-permute-start(bf16[264,4,128]{2,0,1:T(8,128)(2,1)S(1)} %pad_maximum_fusion.4), channel_id=1, source_target_pairs={{0,12},{4,0},{8,4},{12,8},{1,13},{5,1},{9,5},{13,9},{2,14},{6,2},{... | collective-permute-start | bytes 811016 | tf_op jit(solution)/shard_map/ppermute | solution.py:170
  21.0 13.7 %collective-permute-start.3 = (bf16[264,4,128]{2,0,1:T(8,128)(2,1)S(1)}, bf16[264,4,128]{2,0,1:T(8,128)(2,1)S(1)}, u32[]{:S(2)}, u32[]{:S(2)}) collective-permute-start(bf16[264,4,128]{2,0,1:T(8,128)(2,1)S(1)} %pad_maximum_fusion.4), channel_id=1, source_target_pairs={{0,4},{4,8},{8,12},{12,0},{1,5},{5,9},{9,13},{13,1},{2,6},{6,10},{... | collective-permute-start | bytes 811016 | tf_op jit(solution)/shard_map/ppermute | solution.py:170
  21.0 21.9 %collective-permute-start.5 = (bf16[256,4,128]{2,0,1:T(8,128)(2,1)S(1)}, bf16[256,4,128]{2,0,1:T(8,128)(2,1)S(1)}, u32[]{:S(2)}, u32[]{:S(2)}) collective-permute-start(bf16[256,4,128]{2,0,1:T(8,128)(2,1)S(1)} %bitcast.225), channel_id=1, source_target_pairs={{0,8},{4,12},{8,0},{12,4},{1,9},{5,13},{9,1},{13,5},{2,10},{6,14},... | collective-permute-start | bytes 786440 | tf_op jit(solution)/shard_map/ppermute | solution.py:170
  43.9 1.0 copy-start.1
  45.3 1.4 %copy-start.2 = (f32[2,9,128]{2,0,1:T(2,128)S(1)}, f32[2,9,128]{2,0,1:T(2,128)}, u32[]{:S(2)}) copy-start(f32[2,9,128]{2,0,1:T(2,128)} %param.24) | copy-start | bytes 27652
  46.5 1.6 %collective-permute-start.6 = (bf16[2,128,528]{1,2,0:T(8,128)(2,1)S(1)}, bf16[2,128,528]{1,2,0:T(8,128)(2,1)S(1)}, u32[]{:S(2)}, u32[]{:S(2)}) collective-permute-start(bf16[2,128,528]{1,2,0:T(8,128)(2,1)S(1)} %fusion.81), channel_id=1, source_target_pairs={{0,1},{1,0},{2,3},{3,2},{4,5},{5,4},{6,7},{7,6},{8,9},{9,8},{10,11... | collective-permute-start | bytes 811016 | tf_op jit(solution)/shard_map/ppermute | solution.py:64
  48.2 5.7 %collective-permute-start.7 = (bf16[128,528]{0,1:T(8,128)(2,1)S(1)}, bf16[128,528]{0,1:T(8,128)(2,1)S(1)}, u32[]{:S(2)}, u32[]{:S(2)}) collective-permute-start(bf16[128,528]{0,1:T(8,128)(2,1)S(1)} %bitcast_convert_fusion), channel_id=1, source_target_pairs={{0,2},{1,3},{2,0},{3,1},{4,6},{5,7},{6,4},{7,5},{8,10},{9,11},{10,... | collective-permute-start | bytes 405512 | tf_op jit(solution)/shard_map/ppermute | solution.py:71
  54.0 5.4 %copy-start.3 = (f32[2,512]{1,0:T(2,128)S(1)}, f32[2,512]{1,0:T(2,128)}, u32[]{:S(2)}) copy-start(f32[2,512]{1,0:T(2,128)} %param.25) | copy-start | bytes 12292
  54.3 5.0 %collective-permute-start.8 = (bf16[128,520]{0,1:T(8,128)(2,1)S(1)}, bf16[128,520]{0,1:T(8,128)(2,1)S(1)}, u32[]{:S(2)}, u32[]{:S(2)}) collective-permute-start(bf16[128,520]{0,1:T(8,128)(2,1)S(1)} %reshape.783), channel_id=1, source_target_pairs={{0,1},{1,2},{2,3},{3,0},{4,5},{5,6},{6,7},{7,4},{8,9},{9,10},{10,1... | collective-permute-start | bytes 399368 | tf_op jit(solution)/shard_map/ppermute | solution.py:29
  54.4 5.0 %collective-permute-start.10 = (bf16[128,520]{0,1:T(8,128)(2,1)S(1)}, bf16[128,520]{0,1:T(8,128)(2,1)S(1)}, u32[]{:S(2)}, u32[]{:S(2)}) collective-permute-start(bf16[128,520]{0,1:T(8,128)(2,1)S(1)} %reshape.783), channel_id=1, source_target_pairs={{1,0},{2,1},{3,2},{0,3},{5,4},{6,5},{7,6},{4,7},{9,8},{10,9},{11,1... | collective-permute-start | bytes 399368 | tf_op jit(solution)/shard_map/ppermute | solution.py:31
  59.4 4.4 %collective-permute-start.9 = (bf16[128,520]{0,1:T(8,128)(2,1)S(1)}, bf16[128,520]{0,1:T(8,128)(2,1)S(1)}, u32[]{:S(2)}, u32[]{:S(2)}) collective-permute-start(bf16[128,520]{0,1:T(8,128)(2,1)S(1)} %collective-permute-done.8), channel_id=1, source_target_pairs={{0,1},{1,2},{2,3},{3,0},{4,5},{5,6},{6,7},{7,4},{8,9},{9,10},{10,1... | collective-permute-start | bytes 399368 | tf_op jit(solution)/shard_map/ppermute | solution.py:29
  63.9 1.2 %copy-start.5 = (bf16[2,512,512]{2,1,0:T(8,128)(2,1)S(1)}, bf16[2,512,512]{2,1,0:T(8,128)(2,1)}, u32[]{:S(2)}) copy-start(bf16[2,512,512]{2,1,0:T(8,128)(2,1)} %param.27) | copy-start | bytes 3145732
  68.4 1.6 %collective-permute-start.11 = (bf16[2,128,520]{1,2,0:T(8,128)(2,1)S(1)}, bf16[2,128,520]{1,2,0:T(8,128)(2,1)S(1)}, u32[]{:S(2)}, u32[]{:S(2)}) collective-permute-start(bf16[2,128,520]{1,2,0:T(8,128)(2,1)S(1)} %fusion.83), channel_id=1, source_target_pairs={{0,1},{1,0},{2,3},{3,2},{4,5},{5,4},{6,7},{7,6},{8,9},{9,8},{10,11... | collective-permute-start | bytes 798728 | tf_op jit(solution)/shard_map/ppermute | solution.py:64
  70.2 5.6 %collective-permute-start.12 = (bf16[128,520]{0,1:T(8,128)(2,1)S(1)}, bf16[128,520]{0,1:T(8,128)(2,1)S(1)}, u32[]{:S(2)}, u32[]{:S(2)}) collective-permute-start(bf16[128,520]{0,1:T(8,128)(2,1)S(1)} %bitcast_convert_fusion.1), channel_id=1, source_target_pairs={{0,2},{1,3},{2,0},{3,1},{4,6},{5,7},{6,4},{7,5},{8,10},{9,11},{10,... | collective-permute-start | bytes 399368 | tf_op jit(solution)/shard_map/ppermute | solution.py:71
  76.2 5.3 %collective-permute-start.13 = (bf16[128,512]{1,0:T(8,128)(2,1)S(1)}, bf16[128,512]{1,0:T(8,128)(2,1)S(1)}, u32[]{:S(2)}, u32[]{:S(2)}) collective-permute-start(bf16[128,512]{1,0:T(8,128)(2,1)S(1)} %copy.199), channel_id=1, source_target_pairs={{0,1},{1,2},{2,3},{3,0},{4,5},{5,6},{6,7},{7,4},{8,9},{9,10},{10,1... | collective-permute-start | bytes 393224 | tf_op jit(solution)/shard_map/ppermute | solution.py:29
  76.3 5.4 %collective-permute-start.15 = (bf16[128,512]{1,0:T(8,128)(2,1)S(1)}, bf16[128,512]{1,0:T(8,128)(2,1)S(1)}, u32[]{:S(2)}, u32[]{:S(2)}) collective-permute-start(bf16[128,512]{1,0:T(8,128)(2,1)S(1)} %copy.199), channel_id=1, source_target_pairs={{1,0},{2,1},{3,2},{0,3},{5,4},{6,5},{7,6},{4,7},{9,8},{10,9},{11,1... | collective-permute-start | bytes 393224 | tf_op jit(solution)/shard_map/ppermute | solution.py:31
  81.5 4.4 %collective-permute-start.14 = (bf16[128,512]{1,0:T(8,128)(2,1)S(1)}, bf16[128,512]{1,0:T(8,128)(2,1)S(1)}, u32[]{:S(2)}, u32[]{:S(2)}) collective-permute-start(bf16[128,512]{1,0:T(8,128)(2,1)S(1)} %collective-permute-done.13), channel_id=1, source_target_pairs={{0,1},{1,2},{2,3},{3,0},{4,5},{5,6},{6,7},{7,4},{8,9},{9,10},{10,1... | collective-permute-start | bytes 393224 | tf_op jit(solution)/shard_map/ppermute | solution.py:29
  89.0 1.6 %collective-permute-start.16 = (bf16[2,128,512]{2,1,0:T(8,128)(2,1)S(1)}, bf16[2,128,512]{2,1,0:T(8,128)(2,1)S(1)}, u32[]{:S(2)}, u32[]{:S(2)}) collective-permute-start(bf16[2,128,512]{2,1,0:T(8,128)(2,1)S(1)} %select_bitcast_fusion), channel_id=1, source_target_pairs={{0,1},{1,0},{2,3},{3,2},{4,5},{5,4},{6,7},{7,6},{8,9},{9,8},{10,11... | collective-permute-start | bytes 786440 | tf_op jit(solution)/shard_map/ppermute | solution.py:64
  90.7 5.6 %collective-permute-start.17 = (bf16[128,512]{1,0:T(8,128)(2,1)S(1)}, bf16[128,512]{1,0:T(8,128)(2,1)S(1)}, u32[]{:S(2)}, u32[]{:S(2)}) collective-permute-start(bf16[128,512]{1,0:T(8,128)(2,1)S(1)} %bitcast_convert_fusion.2), channel_id=1, source_target_pairs={{0,2},{1,3},{2,0},{3,1},{4,6},{5,7},{6,4},{7,5},{8,10},{9,11},{10,... | collective-permute-start | bytes 393224 | tf_op jit(solution)/shard_map/ppermute | solution.py:71
